TPU v7x, 512 devices: a whole 4x8x8 slice. The times are simulated.
512 devices in a mesh: ctx: 32 (over z, x), tp: 16 (over y, core).
Axes of the slice: x: 4, y: 8, z: 8, core: 2. Of those that a mesh axis runs over, the one named last changes fastest.
Arguments:
- hidden: bfloat16 [8192, 2048], P(('ctx', 'tp')), may hold values from -14 to 14
- in_weight: bfloat16 [2048, 2, 4096], P(None, None, 'tp'), may hold values from -0.125 to 0.125
- step_weight: bfloat16 [2048, 64], P(None, 'tp'), may hold values from -0.125 to 0.125
- group_weight: bfloat16 [256, 4, 2048], P('tp'), may hold values from -0.125 to 0.125
- conv_inner: float32 [4, 4096], P(None, 'tp'), may hold values from -3 to 3
- inner_bias: float32 [4096], P('tp'), may hold values from -2.5 to 2.5
- conv_group: float32 [4, 1024], replicated, may hold values from -3 to 3
- group_bias: float32 [1024], replicated, may hold values from -2.5 to 2.5
- step_bias: float32 [64], P('tp'), may hold values from -9.5 to 0
- log_rate: float32 [64], P('tp'), may hold values from -2.5 to -0.5
- skip_weight: float32 [64], P('tp'), may hold values from 0.25 to 1
- norm_gain: float32 [4096], P('tp'), may hold values from 0.1 to 1.9
- out_weight: bfloat16 [4096, 2048], P('tp'), may hold values from -0.09375 to 0.09375
Outputs:
- mixed: bfloat16 [8192, 2048], P(('ctx', 'tp'))
All inputs are finite; a program needn't handle non-finite values.
Results may differ from a plain program's by a relative error of at most 0.024.
Values may be sent and summed in bfloat16 or wider, within the bound.
No kernel may reach another device: no remote copies, remote signals or barrier semaphores. Data moves between devices by JAX's collectives and lax.ppermute only.
A program may use at most 64 MiB of HBM per device.

v0:
```python
import jax
import jax.numpy as jnp
from jax import lax
from jax.sharding import PartitionSpec as P

HEADS = 64
HEAD_DIM = 64
STATE = 128
GROUPS = 4
BLOCK = 256
KERNEL = 4


def shifted(x, axis, by):
    peers = lax.axis_size(axis)
    pairs = [(i, i + by) for i in range(peers) if 0 <= i + by < peers]
    return lax.ppermute(x, axis, pairs)


def entering(x, axis, combine, identity):
    peers, place = (lax.axis_size(axis), lax.axis_index(axis))
    everything = jax.tree.map(lambda part: lax.all_gather(part, axis), x)
    start = jax.tree.map(
        lambda part, zero: jnp.broadcast_to(jnp.asarray(zero, part.dtype), part.shape), x, identity
    )

    def turn(k, before):
        reached = k < place
        new = combine(before, jax.tree.map(lambda part: part[k], everything))
        return jax.tree.map(lambda a, b: jnp.where(reached, a, b), new, before)

    return lax.fori_loop(0, peers, turn, start)


def causal_conv(prior_rows, raw_rows, conv_weight, conv_bias):
    joined = jnp.concatenate([prior_rows, raw_rows], axis=0).astype(jnp.float32)
    length = raw_rows.shape[0]
    running = jnp.broadcast_to(conv_bias[None, :], raw_rows.shape)
    for offset in range(conv_weight.shape[0]):
        running = running + conv_weight[offset][None, :] * joined[offset : offset + length]
    return jax.nn.silu(running).astype(jnp.bfloat16)


def combine_states(earlier, latter):
    return (earlier[0] * latter[0], latter[0][:, None, None] * earlier[1] + latter[1])


def body(
    hidden,
    in_weight,
    step_weight,
    group_weight,
    conv_inner,
    inner_bias,
    conv_group,
    group_bias,
    step_bias,
    log_rate,
    skip_weight,
    norm_gain,
    out_weight,
):
    heads_dev = log_rate.shape[0]
    inner_dev = in_weight.shape[2]
    group_cols = 2 * STATE
    group_index = lax.axis_index("tp") * heads_dev // (HEADS // GROUPS)
    zx_weight = in_weight.reshape(in_weight.shape[0], 2 * inner_dev)
    full_weight = lax.all_gather(group_weight, "tp", axis=0, tiled=True)
    map_weight = lax.dynamic_slice_in_dim(full_weight, group_index, 1, 1)[:, 0, :]
    shard_rows = lax.all_gather(hidden, "tp", axis=0, tiled=True)
    projected = jnp.concatenate(
        [
            jnp.dot(shard_rows, zx_weight, preferred_element_type=jnp.float32),
            lax.dot_general(
                shard_rows, map_weight, (((1,), (1,)), ((), ())), preferred_element_type=jnp.float32
            ),
            jnp.dot(shard_rows, step_weight, preferred_element_type=jnp.float32),
        ],
        axis=1,
    ).astype(jnp.bfloat16)
    gate_raw = projected[:, :inner_dev]
    inner_raw = projected[:, inner_dev : 2 * inner_dev]
    map_part = projected[:, 2 * inner_dev : projected.shape[1] - heads_dev]
    step_raw = projected[:, projected.shape[1] - heads_dev :]
    border_rows = KERNEL - 1
    length = inner_raw.shape[0]
    inner_prior, map_prior = shifted(
        (inner_raw[length - border_rows :], map_part[length - border_rows :]), "ctx", 1
    )
    x_conv = causal_conv(inner_prior, inner_raw, conv_inner, inner_bias)
    own_taps = lax.dynamic_slice_in_dim(conv_group, group_index * group_cols, group_cols, 1)
    own_bias = lax.dynamic_slice_in_dim(group_bias, group_index * group_cols, group_cols, 0)
    maps = causal_conv(map_prior, map_part, own_taps, own_bias)
    step_size = jax.nn.softplus(step_raw.astype(jnp.float32) + step_bias[None, :])
    decay_rate = -jnp.exp(log_rate)
    blocks = length // BLOCK
    x_blocks = x_conv.reshape(blocks, BLOCK, heads_dev, HEAD_DIM)
    input_map = maps[:, :STATE].reshape(blocks, BLOCK, STATE)
    output_map = maps[:, STATE:].reshape(blocks, BLOCK, STATE)
    step_blocks = jnp.swapaxes(step_size.reshape(blocks, BLOCK, heads_dev), 1, 2)
    cumulative = jnp.cumsum(step_blocks * decay_rate[None, :, None], axis=2)
    scores = jnp.einsum("kin,kjn->kij", output_map, input_map, preferred_element_type=jnp.float32)
    causal = jnp.arange(BLOCK)[:, None] >= jnp.arange(BLOCK)[None, :]
    exponent = jnp.where(causal, cumulative[..., :, None] - cumulative[..., None, :], -jnp.inf)
    mixing = (scores[:, None] * jnp.exp(exponent) * step_blocks[..., None, :]).astype(jnp.bfloat16)
    within = jnp.einsum("khij,kjhp->kihp", mixing, x_blocks, preferred_element_type=jnp.float32)
    weight = jnp.exp(cumulative[..., BLOCK - 1 :] - cumulative) * step_blocks
    x_float = x_blocks.astype(jnp.float32)
    weighted = (x_float * jnp.swapaxes(weight, 1, 2)[..., None]).astype(jnp.bfloat16)
    block_state = jnp.einsum(
        "kjhp,kjn->khpn", weighted, input_map, preferred_element_type=jnp.float32
    )
    block_decay = jnp.exp(cumulative[..., BLOCK - 1])

    def advance(carry, item):
        running, product = carry
        block_stop_index, state_here = item
        return (
            (block_stop_index[:, None, None] * running + state_here, product * block_stop_index),
            (running, product),
        )

    empty_state = jnp.zeros((heads_dev, HEAD_DIM, STATE), jnp.float32)
    (dev_state, dev_decay), (local_starts, prefixes) = lax.scan(
        advance, (empty_state, jnp.ones((heads_dev,), jnp.float32)), (block_decay, block_state)
    )
    decay_in, incoming = entering(
        (dev_decay, dev_state),
        "ctx",
        combine_states,
        (jnp.ones_like(dev_decay), jnp.zeros_like(dev_state)),
    )
    starting = local_starts + prefixes[:, :, None, None] * incoming[None]
    carried = jnp.einsum(
        "kin,khpn->kihp",
        output_map,
        starting.astype(jnp.bfloat16),
        preferred_element_type=jnp.float32,
    )
    carried = carried * jnp.swapaxes(jnp.exp(cumulative), 1, 2)[..., None]
    result_heads = within + carried + skip_weight[None, None, :, None] * x_float
    result_heads = result_heads.reshape(length, inner_dev)
    gated = result_heads * jax.nn.silu(gate_raw.astype(jnp.float32))
    squares = jnp.sum(gated * gated, axis=1)
    own_slot = (jnp.arange(GROUPS) == group_index)[:, None]
    group_sums = lax.psum(jnp.where(own_slot, squares[None, :], 0.0), "tp")
    own_total = jnp.sum(jnp.where(own_slot, group_sums, 0.0), axis=0)
    inverse = lax.rsqrt(own_total / (HEADS * HEAD_DIM // GROUPS) + 1e-05)
    normed = (gated * inverse[:, None] * norm_gain[None, :]).astype(jnp.bfloat16)
    mixed = lax.psum_scatter(
        jnp.dot(normed, out_weight, preferred_element_type=jnp.float32),
        "tp",
        scatter_dimension=0,
        tiled=True,
    )
    return mixed.astype(jnp.bfloat16)


def solution(mesh):
    placed = (
        P(("ctx", "tp"), None),
        P(None, None, "tp"),
        P(None, "tp"),
        P("tp", None, None),
        P(None, "tp"),
        P("tp"),
        P(),
        P(),
        P("tp"),
        P("tp"),
        P("tp"),
        P("tp"),
        P("tp", None),
    )
    return jax.shard_map(
        body, mesh=mesh, in_specs=placed, out_specs=P(("ctx", "tp"), None), check_vma=False
    )
```

profile of v0, /device:TPU:27, one launch (start us, length us, event | category | flops | bytes accessed | tf_op | source)
XLA Modules:
  0.0 323.9 jit_solution(4867282855328708421)
XLA Ops:
  7.3 1.8 copy.45
  9.3 2.1 copy.56
  13.1 41.7 %all-gather.6.cloned.1.call-done = bf16[256,2048]{1,0:T(8,128)(2,1)} async-done(((bf16[16,2048]{1,0:T(8,128)(2,1)}), bf16[256,2048]{1,0:T(8,128)(2,1)}) %all-gather.6.cloned.1.call-update) | async-done | bytes 1048592 | tf_op jit(solution)/shard_map/all_gather | solution.py:70
  54.8 1.6 bitcast_multiply_fusion.1
  56.4 1.2 reduce-window.6
  58.1 1.9 convolution_convert_fusion
  60.1 3.1 collective-permute-start
  64.4 35.8 %all-gather.8.cloned.1.call-done = bf16[256,4,2048]{2,0,1:T(8,128)(2,1)} async-done(((bf16[16,4,2048]{2,0,1:T(8,128)(2,1)}), bf16[256,4,2048]{2,0,1:T(8,128)(2,1)}) %all-gather.8.cloned.1.call-update) | async-done | bytes 4194320 | tf_op jit(solution)/shard_map/all_gather | solution.py:68
  100.3 2.0 fusion.4
  102.3 3.1 collective-permute-start.1
  107.9 34.2 %all-gather = f32[32,4,1]{1,2,0:T(1,128)S(1)} all-gather(f32[1,4,1]{1,2,0:T(1,128)S(1)} %copy.48), channel_id=2, replica_groups=mesh['ctx'=32,'tp'=16] {'ctx'}, dimensions={0}, use_global_device_ids=true | all-gather | bytes 528 | tf_op jit(solution)/shard_map/all_gather | solution.py:22
  142.6 49.1 %all-gather.10.cloned.1.call-done = f32[128,64,128]{2,1,0:T(8,128)} async-done(((f32[4,64,128]{2,1,0:T(8,128)}), f32[128,64,128]{2,1,0:T(8,128)}) %all-gather.10.cloned.1.call-update) | async-done | bytes 4194320 | tf_op jit(solution)/shard_map/all_gather | solution.py:22
  191.7 33.1 %while.9 = (s32[]{:T(128)}, f32[4,64,128]{2,1,0:T(8,128)S(1)}, s32[]{:T(128)}, f32[32,4]{1,0:T(8,128)S(1)}, f32[32,4,64,128]{3,2,1,0:T(8,128)}, /*index=5*/s32[]{:T(128)}, s32[]{:T(128)}) while((s32[]{:T(128)}, f32[4,64,128]{2,1,0:T(8,128)S(1)}, s32[]{:T(128)}, f32[32,4]{1,0:T(8,128)S(1)}, f32[32,4,64,128]{3,2,1,0:T(8,128)}, ...), condition=%wide.region_3.4_spmd.clone, body=%wide.region_2.3_spmd.clone.sunk | while | flops 131076 | bytes 393369 | solution.py:32
  192.7 1.0 fusion.52
  193.8 1.0 fusion.52
  194.8 1.0 fusion.52
  195.8 1.0 fusion.52
  196.9 1.0 fusion.52
  197.9 1.0 fusion.52
  198.9 1.0 fusion.52
  200.0 1.0 fusion.52
  201.0 1.0 fusion.52
  202.0 1.0 fusion.52
  203.1 1.0 fusion.52
  204.1 1.0 fusion.52
  205.1 1.0 fusion.52
  206.2 1.0 fusion.52
  207.2 1.0 fusion.52
  225.8 26.8 %psum.7 = f32[4,256]{1,0:T(4,128)S(1)} all-reduce(f32[4,256]{1,0:T(4,128)S(1)} %broadcast_select_fusion), channel_id=1, replica_groups=mesh['ctx'=32,'tp'=16] {'tp'}, use_global_device_ids=true, to_apply=%region_5.6 | all-reduce | flops 1024 | bytes 8192 | tf_op jit(solution)/shard_map/psum | solution.py:146
  252.8 1.8 fusion.27
  254.7 61.1 %reduce-scatter.2.cloned.1.call-done = f32[16,2048]{1,0:T(8,128)} async-done(((f32[256,2048]{1,0:T(8,128)}), f32[16,2048]{1,0:T(8,128)}) %reduce-scatter.2.cloned.1.call-update) | async-done | bytes 131088 | tf_op jit(solution)/shard_map/reduce_scatter | solution.py:150
  315.8 1.5 convert_element_type.77
  (119 shorter events, 25.4 us)
Async XLA Ops:
  6.5 246.2 %copy-start = (bf16[256,2048]{1,0:T(8,128)(2,1)S(1)}, bf16[256,2048]{1,0:T(8,128)(2,1)}, u32[]{:S(2)}) copy-start(bf16[256,2048]{1,0:T(8,128)(2,1)} %param.27) | copy-start | bytes 3145732
  6.5 48.3 %all-gather.6.cloned.1.call-start = ((), (), s32[]{:S(2)}) async-start(), calls=%async_computation.1 | async-start | bytes 1114112 | tf_op jit(solution)/shard_map/all_gather | solution.py:70
  7.3 93.0 %all-gather.8.cloned.1.call-start = ((), (), s32[]{:S(2)}) async-start(), calls=%async_computation.2 | async-start | bytes 4456448 | tf_op jit(solution)/shard_map/all_gather | solution.py:68
  9.2 182.5 %all-gather.10.cloned.1.call-start = ((), (), s32[]{:S(2)}) async-start(), calls=%async_computation.4 | async-start | bytes 4325376 | tf_op jit(solution)/shard_map/all_gather | solution.py:22
  9.2 3.8 %copy-start.5 = (f32[4]{0:T(128)S(1)}, f32[4]{0:T(128)}, u32[]{:S(2)}) copy-start(f32[4]{0:T(128)} %param.24) | copy-start | bytes 52
  9.2 3.8 %copy-start.1 = (f32[4,256]{1,0:T(4,128)S(1)}, f32[4,256]{1,0:T(4,128)}, u32[]{:S(2)}) copy-start(f32[4,256]{1,0:T(4,128)} %param.19) | copy-start | bytes 12292
  9.3 45.5 %copy-start.4 = (bf16[2048,4]{0,1:T(4,128)(2,1)S(1)}, bf16[2048,4]{0,1:T(4,128)(2,1)}, u32[]{:S(2)}) copy-start(bf16[2048,4]{0,1:T(4,128)(2,1)} %param.17) | copy-start | bytes 49156
  9.3 45.5 %copy-start.6 = (f32[4]{0:T(128)S(1)}, f32[4]{0:T(128)}, u32[]{:S(2)}) copy-start(f32[4]{0:T(128)} %param.23) | copy-start | bytes 52
  60.0 45.4 %copy-start.3 = (f32[256]{0:T(256)S(1)}, f32[256]{0:T(256)}, u32[]{:S(2)}) copy-start(f32[256]{0:T(256)} %param.20) | copy-start | bytes 3076
  60.1 4.3 %collective-permute-start = (bf16[3,256]{1,0:T(4,128)(2,1)S(1)}, bf16[3,256]{1,0:T(4,128)(2,1)S(1)}, u32[]{:S(2)}, u32[]{:S(2)}) collective-permute-start(bf16[3,256]{1,0:T(4,128)(2,1)S(1)} %slice.112), channel_id=1, source_target_pairs={{0,16},{16,32},{32,48},{48,64},{64,80},{80,96},{96,112},{112,128},... | collective-permute-start | bytes 4616 | tf_op jit(solution)/shard_map/ppermute | solution.py:17
  102.3 4.3 %collective-permute-start.1 = (bf16[3,256]{1,0:T(4,128)(2,1)S(1)}, bf16[3,256]{1,0:T(4,128)(2,1)S(1)}, u32[]{:S(2)}, u32[]{:S(2)}) collective-permute-start(bf16[3,256]{1,0:T(4,128)(2,1)S(1)} %slice.118), channel_id=1, source_target_pairs={{0,16},{16,32},{32,48},{48,64},{64,80},{80,96},{96,112},{112,128},... | collective-permute-start | bytes 4616 | tf_op jit(solution)/shard_map/ppermute | solution.py:17
  106.8 118.1 %copy-start.7 = (f32[4]{0:T(128)S(1)}, f32[4]{0:T(128)}, u32[]{:S(2)}) copy-start(f32[4]{0:T(128)} %param.25) | copy-start | bytes 52
  107.7 208.1 %reduce-scatter.2.cloned.1.call-start = ((), (), s32[]{:S(2)}) async-start(), calls=%async_computation.3 | async-start | bytes 2228224 | tf_op jit(solution)/shard_map/reduce_scatter | solution.py:150
  224.8 28.0 %copy-start.2 = (f32[256]{0:T(256)S(1)}, f32[256]{0:T(256)}, u32[]{:S(2)}) copy-start(f32[256]{0:T(256)} %param.26) | copy-start | bytes 3076
Sparse Core Ops, SparseCore 0:
  9.5 45.2 all-gather.5
  56.9 43.2 all-gather.7
  107.8 83.8 all-gather.9
  254.8 60.9 reduce-scatter.1
where the time goes:
time: 325 us; the launch traced here: 324 us
  waiting for transfers between devices  190 us (58%)
  blocking collectives  61.1 us (19%)
  other arithmetic  35.5 us (11%)
  between operations  13.5 us (4%)
  matrix products  9.08 us (3%)
  local copies, waits for them, and re-layouts  7.25 us (2%)
  starting transfers between devices  6.32 us (2%)
    reduce_scatter x1, waiting for transfers between devices, body(): lax.psum_scatter(jnp.dot(normed, out_weight, preferred_element_type=jnp.f...  61.1 us
    all_gather x1, waiting for transfers between devices, entering(): everything = jax.tree.map(lambda part: lax.all_gather(part, axis), x)  49.1 us
    all_gather x1, waiting for transfers between devices, body(): shard_rows = lax.all_gather(hidden, 'tp', axis=0, tiled=True)  41.7 us
    all_gather x1, waiting for transfers between devices, body(): full_weight = lax.all_gather(group_weight, 'tp', axis=0, tiled=True)  35.8 us
    all_gather x1, blocking collectives, entering(): everything = jax.tree.map(lambda part: lax.all_gather(part, axis), x)  34.2 us
    select_n x32, other arithmetic, turn(): return jax.tree.map(lambda a, b: jnp.where(reached, a, b), new, before)  31.8 us
    psum x1, blocking collectives, body(): group_sums = lax.psum(jnp.where(own_slot, squares[None, :], 0.0), 'tp')  26.8 us
  transfers between devices with their start and end apart: 6, of which 6 were waited for; matrix products, arithmetic and copies ran while one was open for 4% of the time, Pallas kernels for 0%

commit v1 on v0

--- a/solution.py
+++ b/solution.py
@@ -143,7 +143,7 @@
     gated = result_heads * jax.nn.silu(gate_raw.astype(jnp.float32))
     squares = jnp.sum(gated * gated, axis=1)
     own_slot = (jnp.arange(GROUPS) == group_index)[:, None]
-    group_sums = lax.psum(jnp.where(own_slot, squares[None, :], 0.0), "tp")
+    group_sums = jnp.sum(lax.all_gather(jnp.where(own_slot, squares[None, :], 0.0), "tp"), axis=0)
     own_total = jnp.sum(jnp.where(own_slot, group_sums, 0.0), axis=0)
     inverse = lax.rsqrt(own_total / (HEADS * HEAD_DIM // GROUPS) + 1e-05)
     normed = (gated * inverse[:, None] * norm_gain[None, :]).astype(jnp.bfloat16)

time: 325 us -> 316 us (0.972)
  the two profiles are of different devices: /device:TPU:27 before, /device:TPU:25 now
where the time goes in v1:
time: 316 us; the launch traced here: 315 us
  waiting for transfers between devices  188 us (59%)
  blocking collectives  55 us (17%)
  other arithmetic  35.5 us (11%)
  between operations  13.5 us (4%)
  matrix products  9.07 us (3%)
  local copies, waits for them, and re-layouts  7.25 us (2%)
  starting transfers between devices  6.31 us (2%)
    reduce_scatter x1, waiting for transfers between devices, body(): lax.psum_scatter(jnp.dot(normed, out_weight, preferred_element_type=jnp.f...  57.9 us
    all_gather x1, waiting for transfers between devices, entering(): everything = jax.tree.map(lambda part: lax.all_gather(part, axis), x)  50.2 us
    all_gather x1, waiting for transfers between devices, body(): shard_rows = lax.all_gather(hidden, 'tp', axis=0, tiled=True)  41.8 us
    all_gather x1, waiting for transfers between devices, body(): full_weight = lax.all_gather(group_weight, 'tp', axis=0, tiled=True)  36.4 us
    all_gather x1, blocking collectives, entering(): everything = jax.tree.map(lambda part: lax.all_gather(part, axis), x)  35 us
    select_n x32, other arithmetic, turn(): return jax.tree.map(lambda a, b: jnp.where(reached, a, b), new, before)  31.8 us
    all_gather x1, blocking collectives, body(): lax.all_gather(jnp.where(own_slot, squares[None, :], 0.0), 'tp')  19.9 us
  transfers between devices with their start and end apart: 6, of which 6 were waited for; matrix products, arithmetic and copies ran while one was open for 4% of the time, Pallas kernels for 0%

profile of v1, /device:TPU:25, one launch (start us, length us, event | category | flops | bytes accessed | tf_op | source)
XLA Modules:
  0.0 315.1 jit_solution(14342866990122628371)
XLA Ops:
  7.3 1.8 copy.45
  9.3 2.1 copy.56
  13.1 41.8 %all-gather.6.cloned.1.call-done = bf16[256,2048]{1,0:T(8,128)(2,1)} async-done(((bf16[16,2048]{1,0:T(8,128)(2,1)}), bf16[256,2048]{1,0:T(8,128)(2,1)}) %all-gather.6.cloned.1.call-update) | async-done | bytes 1048592 | tf_op jit(solution)/shard_map/all_gather | solution.py:70
  54.8 1.6 bitcast_multiply_fusion.1
  56.5 1.2 reduce-window.6
  58.1 1.9 convolution_convert_fusion
  60.1 3.1 collective-permute-start
  63.9 36.4 %all-gather.8.cloned.1.call-done = bf16[256,4,2048]{2,0,1:T(8,128)(2,1)} async-done(((bf16[16,4,2048]{2,0,1:T(8,128)(2,1)}), bf16[256,4,2048]{2,0,1:T(8,128)(2,1)}) %all-gather.8.cloned.1.call-update) | async-done | bytes 4194320 | tf_op jit(solution)/shard_map/all_gather | solution.py:68
  100.3 2.0 fusion.4
  102.3 3.1 collective-permute-start.1
  107.4 35.0 %all-gather = f32[32,4,1]{1,2,0:T(1,128)S(1)} all-gather(f32[1,4,1]{1,2,0:T(1,128)S(1)} %copy.48), channel_id=2, replica_groups=mesh['ctx'=32,'tp'=16] {'ctx'}, dimensions={0}, use_global_device_ids=true | all-gather | bytes 528 | tf_op jit(solution)/shard_map/all_gather | solution.py:22
  142.9 50.2 %all-gather.10.cloned.1.call-done = f32[128,64,128]{2,1,0:T(8,128)} async-done(((f32[4,64,128]{2,1,0:T(8,128)}), f32[128,64,128]{2,1,0:T(8,128)}) %all-gather.10.cloned.1.call-update) | async-done | bytes 4194320 | tf_op jit(solution)/shard_map/all_gather | solution.py:22
  193.1 33.1 %while.9 = (s32[]{:T(128)}, f32[4,64,128]{2,1,0:T(8,128)S(1)}, s32[]{:T(128)}, f32[32,4]{1,0:T(8,128)S(1)}, f32[32,4,64,128]{3,2,1,0:T(8,128)}, /*index=5*/s32[]{:T(128)}, s32[]{:T(128)}) while((s32[]{:T(128)}, f32[4,64,128]{2,1,0:T(8,128)S(1)}, s32[]{:T(128)}, f32[32,4]{1,0:T(8,128)S(1)}, f32[32,4,64,128]{3,2,1,0:T(8,128)}, ...), condition=%wide.region_3.4_spmd.clone, body=%wide.region_2.3_spmd.clone.sunk | while | flops 131076 | bytes 393369 | solution.py:32
  194.1 1.0 fusion.52
  195.1 1.0 fusion.52
  197.2 1.0 fusion.52
  199.3 1.0 fusion.52
  200.3 1.0 fusion.52
  201.4 1.0 fusion.52
  202.4 1.0 fusion.52
  203.4 1.0 fusion.52
  204.5 1.0 fusion.52
  205.5 1.0 fusion.52
  206.5 1.0 fusion.52
  207.6 1.0 fusion.52
  208.6 1.0 fusion.52
  209.6 1.0 fusion.52
  210.7 1.0 fusion.52
  227.2 19.9 %all_gather.22 = f32[16,4,256]{2,1,0:T(4,128)S(1)} all-gather(f32[1,4,256]{2,1,0:T(4,128)S(1)} %broadcast_select_fusion), channel_id=1, replica_groups=mesh['ctx'=32,'tp'=16] {'tp'}, dimensions={0}, use_global_device_ids=true | all-gather | bytes 69632 | tf_op jit(solution)/shard_map/all_gather | solution.py:146
  247.3 1.8 fusion.27
  249.2 57.9 %reduce-scatter.2.cloned.1.call-done = f32[16,2048]{1,0:T(8,128)} async-done(((f32[256,2048]{1,0:T(8,128)}), f32[16,2048]{1,0:T(8,128)}) %reduce-scatter.2.cloned.1.call-update) | async-done | bytes 131088 | tf_op jit(solution)/shard_map/reduce_scatter | solution.py:150
  307.0 1.5 convert_element_type.77
  (120 shorter events, 24.4 us)
Async XLA Ops:
  6.5 240.8 %copy-start = (bf16[256,2048]{1,0:T(8,128)(2,1)S(1)}, bf16[256,2048]{1,0:T(8,128)(2,1)}, u32[]{:S(2)}) copy-start(bf16[256,2048]{1,0:T(8,128)(2,1)} %param.27) | copy-start | bytes 3145732
  6.5 48.3 %all-gather.6.cloned.1.call-start = ((), (), s32[]{:S(2)}) async-start(), calls=%async_computation.1 | async-start | bytes 1114112 | tf_op jit(solution)/shard_map/all_gather | solution.py:70
  7.3 93.0 %all-gather.8.cloned.1.call-start = ((), (), s32[]{:S(2)}) async-start(), calls=%async_computation.2 | async-start | bytes 4456448 | tf_op jit(solution)/shard_map/all_gather | solution.py:68
  9.2 183.9 %all-gather.10.cloned.1.call-start = ((), (), s32[]{:S(2)}) async-start(), calls=%async_computation.4 | async-start | bytes 4325376 | tf_op jit(solution)/shard_map/all_gather | solution.py:22
  9.2 3.8 %copy-start.5 = (f32[4]{0:T(128)S(1)}, f32[4]{0:T(128)}, u32[]{:S(2)}) copy-start(f32[4]{0:T(128)} %param.24) | copy-start | bytes 52
  9.2 3.8 %copy-start.1 = (f32[4,256]{1,0:T(4,128)S(1)}, f32[4,256]{1,0:T(4,128)}, u32[]{:S(2)}) copy-start(f32[4,256]{1,0:T(4,128)} %param.19) | copy-start | bytes 12292
  9.3 45.6 %copy-start.4 = (bf16[2048,4]{0,1:T(4,128)(2,1)S(1)}, bf16[2048,4]{0,1:T(4,128)(2,1)}, u32[]{:S(2)}) copy-start(bf16[2048,4]{0,1:T(4,128)(2,1)} %param.17) | copy-start | bytes 49156
  9.3 45.6 %copy-start.6 = (f32[4]{0:T(128)S(1)}, f32[4]{0:T(128)}, u32[]{:S(2)}) copy-start(f32[4]{0:T(128)} %param.23) | copy-start | bytes 52
  60.0 45.4 %copy-start.3 = (f32[256]{0:T(256)S(1)}, f32[256]{0:T(256)}, u32[]{:S(2)}) copy-start(f32[256]{0:T(256)} %param.20) | copy-start | bytes 3076
  60.1 3.8 %collective-permute-start = (bf16[3,256]{1,0:T(4,128)(2,1)S(1)}, bf16[3,256]{1,0:T(4,128)(2,1)S(1)}, u32[]{:S(2)}, u32[]{:S(2)}) collective-permute-start(bf16[3,256]{1,0:T(4,128)(2,1)S(1)} %slice.112), channel_id=1, source_target_pairs={{0,16},{16,32},{32,48},{48,64},{64,80},{80,96},{96,112},{112,128},... | collective-permute-start | bytes 4616 | tf_op jit(solution)/shard_map/ppermute | solution.py:17
  102.3 3.8 %collective-permute-start.1 = (bf16[3,256]{1,0:T(4,128)(2,1)S(1)}, bf16[3,256]{1,0:T(4,128)(2,1)S(1)}, u32[]{:S(2)}, u32[]{:S(2)}) collective-permute-start(bf16[3,256]{1,0:T(4,128)(2,1)S(1)} %slice.118), channel_id=1, source_target_pairs={{0,16},{16,32},{32,48},{48,64},{64,80},{80,96},{96,112},{112,128},... | collective-permute-start | bytes 4616 | tf_op jit(solution)/shard_map/ppermute | solution.py:17
  106.3 120.0 %copy-start.7 = (f32[4]{0:T(128)S(1)}, f32[4]{0:T(128)}, u32[]{:S(2)}) copy-start(f32[4]{0:T(128)} %param.25) | copy-start | bytes 52
  107.2 199.8 %reduce-scatter.2.cloned.1.call-start = ((), (), s32[]{:S(2)}) async-start(), calls=%async_computation.3 | async-start | bytes 2228224 | tf_op jit(solution)/shard_map/reduce_scatter | solution.py:150
  226.1 21.2 %copy-start.2 = (f32[256]{0:T(256)S(1)}, f32[256]{0:T(256)}, u32[]{:S(2)}) copy-start(f32[256]{0:T(256)} %param.26) | copy-start | bytes 3076
Sparse Core Ops, SparseCore 0:
  9.5 45.3 all-gather.5
  57.0 43.2 all-gather.7
  107.3 85.7 all-gather.9
  249.3 57.6 reduce-scatter.1
